TPU v7x, 32 devices: a whole 2x2x4 slice. The times are simulated.
32 devices in a mesh: tensor: 4 (over x, core), replica: 4 (over z), fsdp: 2 (over y).
Axes of the slice: x: 2, y: 2, z: 4, core: 2. Of those that a mesh axis runs over, the one named last changes fastest.
Arguments:
- gradients: bfloat16 [4, 128, 28672], P('replica', 'fsdp', 'tensor'), may hold values from -6 to 6
- seeds: int32 [2], replicated, may hold values from 0 to 1073741823
- adam_step: int32 [1], replicated, may hold values from 1 to 8
- first_moment: float32 [128, 28672], P(('fsdp', 'replica'), 'tensor'), may hold values from -0.6 to 0.6
- second_moment: float32 [128, 28672], P(('fsdp', 'replica'), 'tensor'), may hold values from 0.001 to 0.1
Outputs:
- new_first: float32 [128, 28672], P(('fsdp', 'replica'), 'tensor')
- new_second: float32 [128, 28672], P(('fsdp', 'replica'), 'tensor')
- step_update: float32 [128, 28672], P(('fsdp', 'replica'), 'tensor')
All inputs are finite; a program needn't handle non-finite values.
Results may differ from a plain program's by a relative error of at most 0.012.
The roundings to bfloat16 on the way count: a program that leaves them out, or rounds other values in their place, can miss the bound.
Values may be sent and summed in bfloat16 or wider, within the bound.
No kernel may reach another device: no remote copies, remote signals or barrier semaphores. Data moves between devices by JAX's collectives and lax.ppermute only.
A program may use at most 64 MiB of HBM per device.

v0:
```python
import math
import jax
import jax.numpy as jnp
from jax import lax
from jax.sharding import PartitionSpec as P

RANK = 512
GROUP = ("fsdp", "replica")


def scramble(value):
    value = value ^ lax.shift_right_logical(value, jnp.full_like(value, 16))
    value = value * jnp.int32(-2048144789)
    value = value ^ lax.shift_right_logical(value, jnp.full_like(value, 13))
    value = value * jnp.int32(-1028477387)
    value = value ^ lax.shift_right_logical(value, jnp.full_like(value, 16))
    return value


def projection_block(first_column, columns, rank, seeds):
    seed_key = seeds[0] ^ seeds[1] * jnp.int32(668265263)
    column = lax.broadcasted_iota(jnp.int32, (columns, rank), 0) + first_column
    entry = lax.broadcasted_iota(jnp.int32, (columns, rank), 1)
    counter = (column * jnp.int32(rank) + entry) * jnp.int32(2)
    hash_a = scramble(counter * jnp.int32(-1640531535) ^ seed_key)
    hash_b = scramble((counter + jnp.int32(1)) * jnp.int32(-1640531535) ^ seed_key)
    inverse = 1.0 / 16777216.0
    uniform_a = (
        lax.shift_right_logical(hash_a, jnp.full_like(hash_a, 8)).astype(jnp.float32) + 0.5
    ) * inverse
    uniform_b = (
        lax.shift_right_logical(hash_b, jnp.full_like(hash_b, 8)).astype(jnp.float32) + 0.5
    ) * inverse
    gauss = jnp.sqrt(-2.0 * jnp.log(uniform_a)) * jnp.cos(6.283185307179586 * uniform_b)
    return (gauss * rank ** (-0.5)).astype(jnp.bfloat16)


def adam(first_moment, second_moment, estimate, adam_step):
    new_first = 0.9 * first_moment + 0.1 * estimate
    new_second = 0.95 * second_moment + 0.05 * estimate * estimate
    step_float = adam_step[0].astype(jnp.float32)
    fix_first = 1.0 - jnp.power(jnp.float32(0.9), step_float)
    fix_second = 1.0 - jnp.power(jnp.float32(0.95), step_float)
    step_update = new_first / fix_first / (jnp.sqrt(new_second / fix_second) + 1e-08)
    return (new_first, new_second, step_update)


def per_device_whole(gradients, seeds, adam_step, first_moment, second_moment):
    gradient = gradients[0]
    columns = gradient.shape[1]
    replicas = lax.axis_size("replica")
    column_start = lax.axis_index("tensor") * jnp.int32(columns)
    piece_cols = math.gcd(columns, 512)
    blocks = columns // piece_cols
    starts = column_start + lax.iota(jnp.int32, blocks) * jnp.int32(piece_cols)
    tiles = lax.map(lambda first: projection_block(first, piece_cols, RANK, seeds), starts)
    projection = tiles.reshape(columns, RANK)
    partial_value = jnp.dot(gradient, projection, preferred_element_type=jnp.float32) * (
        1.0 / replicas
    )
    share = lax.psum_scatter(partial_value, "replica", scatter_dimension=0, tiled=True)
    sketch = lax.psum(share, "tensor")
    sketch_rounded = sketch.astype(jnp.bfloat16)
    estimate = lax.dot_general(
        sketch_rounded, projection, (((1,), (1,)), ((), ())), preferred_element_type=jnp.float32
    )
    return adam(first_moment, second_moment, estimate, adam_step)


def per_device(gradients, seeds, adam_step, first_moment, second_moment):
    gradient = gradients[0]
    rows, columns = gradient.shape
    n_fsdp = lax.axis_size("fsdp")
    n_rep = lax.axis_size("replica")
    n_group = n_fsdp * n_rep
    width = columns // n_group
    if columns % (n_group * 128) != 0:
        return per_device_whole(gradients, seeds, adam_step, first_moment, second_moment)
    member = lax.axis_index(GROUP)
    first = lax.axis_index("tensor") * jnp.int32(columns) + member * jnp.int32(width)
    projection = lax.optimization_barrier(projection_block(first, width, RANK, seeds))
    pieces = gradient.reshape(rows, n_group, width).transpose(1, 0, 2)
    held = lax.all_to_all(pieces, GROUP, 0, 0, tiled=True)
    held = held.reshape(n_fsdp, n_rep, rows, width)
    partial_value = None
    for r in range(n_rep):
        term = lax.dot_general(
            held[:, r], projection, (((2,), (0,)), ((), ())), preferred_element_type=jnp.float32
        )
        partial_value = term if partial_value is None else partial_value + term
    partial_value = partial_value.reshape(n_fsdp * rows, RANK) * (1.0 / n_rep)
    sketch = lax.psum(partial_value, ("tensor",) + GROUP)
    sketch_rounded = sketch.astype(jnp.bfloat16)
    estimate = lax.dot_general(
        sketch_rounded, projection, (((1,), (1,)), ((), ())), preferred_element_type=jnp.float32
    )
    out_rows = first_moment.shape[0]
    estimate = estimate.reshape(n_group, out_rows, width)
    estimate = lax.all_to_all(estimate, GROUP, 0, 0, tiled=True)
    estimate = estimate.transpose(1, 0, 2).reshape(out_rows, columns)
    return adam(first_moment, second_moment, estimate, adam_step)


def solution(mesh):
    placed = (
        P("replica", "fsdp", "tensor"),
        P(),
        P(),
        P(("fsdp", "replica"), "tensor"),
        P(("fsdp", "replica"), "tensor"),
    )
    return jax.shard_map(
        per_device,
        mesh=mesh,
        in_specs=placed,
        out_specs=(
            P(("fsdp", "replica"), "tensor"),
            P(("fsdp", "replica"), "tensor"),
            P(("fsdp", "replica"), "tensor"),
        ),
        check_vma=False,
    )
```

profile of v0, /device:TPU:0, one launch (start us, length us, event | category | flops | bytes accessed | tf_op | source)
XLA Modules:
  0.0 96.1 jit_solution(1003083572574440337)
XLA Ops:
  0.6 1.3 %copy.31 = bf16[8,8,8,896]{3,2,1,0:T(8,128)(2,1)S(1)} copy(bf16[8,8,8,896]{3,1,2,0:T(8,128)(2,1)} %bitcast.55) | data formatting | bytes 1835008
  2.0 1.1 %copy.20 = bf16[8,64,896]{2,1,0:T(8,128)(2,1)} copy(bf16[8,64,896]{2,0,1:T(8,128)(2,1)S(1)} %bitcast.51) | data formatting | bytes 1835008 | tf_op jit(solution)/shard_map/transpose | solution.py:82
  3.1 0.0 copy-start.2
  3.1 7.4 %all-to-all-start = ((bf16[8,64,896]{2,1,0:T(8,128)(2,1)}), bf16[8,64,896]{2,1,0:T(8,128)(2,1)S(1)}, u32[]{:S(2)}, u32[]{:S(2)}) async-start(bf16[8,64,896]{2,1,0:T(8,128)(2,1)} %copy.20), calls=%async_computation | async-start | bytes 1835008 | tf_op jit(solution)/shard_map/all_to_all | solution.py:83
  10.5 0.0 copy-done.2
  10.5 0.6 fusion.29
  12.4 9.2 %fusion.18 = bf16[896,512]{1,0:T(8,128)(2,1)S(1)} fusion(s32[]{:T(128)} %bitcast, s32[896]{0:T(1024)S(1)} %add_multiply_fusion), kind=kLoop, calls=%fused_computation.24 | loop fusion | flops 16056320 | bytes 921092 | tf_op jit(solution)/shard_map/convert_element_type | solution.py:35
  21.6 12.7 %all-to-all-done = bf16[8,64,896]{2,1,0:T(8,128)(2,1)S(1)} async-done(((bf16[8,64,896]{2,1,0:T(8,128)(2,1)}), bf16[8,64,896]{2,1,0:T(8,128)(2,1)S(1)}, u32[]{:S(2)}, u32[]{:S(2)}) %all-to-all-start) | async-done | bytes 917536 | tf_op jit(solution)/shard_map/all_to_all | solution.py:83
  34.3 0.3 fusion.23
  34.6 0.3 convolution_add_fusion.2
  34.9 0.3 convolution_add_fusion.1
  35.3 0.3 fusion.19
  35.6 40.4 %all-reduce.1 = bf16[128,512]{1,0:T(8,128)(2,1)S(1)} all-reduce(f32[128,512]{1,0:T(8,128)S(1)} %bitcast.54), channel_id=1, replica_groups=mesh['tensor'=4,'replica'=4,'fsdp'=2] {'tensor','fsdp','replica'}, use_global_device_ids=true, to_apply=%region_0.0 | all-reduce | flops 65536 | bytes 393216 | tf_op jit(solution)/shard_map/psum | solution.py:92
  76.0 1.2 %fusion.30 = f32[128,896]{1,0:T(8,128)} fusion(bf16[128,512]{1,0:T(8,128)(2,1)S(1)} %all-reduce.1, bf16[896,512]{1,0:T(8,128)(2,1)S(1)} %fusion.18), kind=kOutput, calls=%fused_computation.46 | convolution fusion | flops 117440512 | bytes 1507328 | tf_op jit(solution)/shard_map/dot_general | solution.py:94
  77.3 0.0 copy-start
  77.3 0.0 copy-start.1
  77.3 4.4 %all-to-all-start.1 = ((f32[8,16,896]{2,1,0:T(8,128)}), f32[8,16,896]{2,1,0:T(8,128)S(1)}, u32[]{:S(2)}, u32[]{:S(2)}) async-start(f32[8,16,896]{2,1,0:T(8,128)} %bitcast.10), calls=%async_computation.1 | async-start | bytes 917504 | tf_op jit(solution)/shard_map/all_to_all | solution.py:99
  82.3 12.4 %all-to-all-done.1 = f32[8,16,896]{2,1,0:T(8,128)S(1)} async-done(((f32[8,16,896]{2,1,0:T(8,128)}), f32[8,16,896]{2,1,0:T(8,128)S(1)}, u32[]{:S(2)}, u32[]{:S(2)}) %all-to-all-start.1) | async-done | bytes 458784 | tf_op jit(solution)/shard_map/all_to_all | solution.py:99
  94.8 0.0 copy-done
  94.8 0.0 copy-done.1
  94.8 1.2 %multiply_divide_fusion = (f32[16,7168]{1,0:T(8,128)}, f32[16,7168]{1,0:T(8,128)}, f32[16,7168]{1,0:T(8,128)}) fusion(f32[]{:T(128)} %bitcast.13, f32[]{:T(128)} %bitcast.12, f32[16,7168]{1,0:T(8,128)S(1)} %bitcast.52, f32[16,7168]{1,0:T(8,128)S(1)} %copy-done, f32[16,7168]{1,0:T(8,128)S(1)} %copy-done.1), kind=kLoop, calls=%fused_computation.36 | loop fusion | flops 1261568 | bytes 2752520 | tf_op jit(solution)/shard_map/div | solution.py:44
  (2 shorter events, 0.0 us)
Async XLA Ops:
  3.1 7.4 %copy-start.2 = (s32[2]{0:T(128)S(1)}, s32[2]{0:T(128)}, u32[]{:S(2)}) copy-start(s32[2]{0:T(128)} %param.6) | copy-start | bytes 28
  3.1 31.3 %all-to-all-start = ((bf16[8,64,896]{2,1,0:T(8,128)(2,1)}), bf16[8,64,896]{2,1,0:T(8,128)(2,1)S(1)}, u32[]{:S(2)}, u32[]{:S(2)}) async-start(bf16[8,64,896]{2,1,0:T(8,128)(2,1)} %copy.20), calls=%async_computation | async-start | bytes 1835008 | tf_op jit(solution)/shard_map/all_to_all | solution.py:83
  77.3 17.6 %copy-start = (f32[16,7168]{1,0:T(8,128)S(1)}, f32[16,7168]{1,0:T(8,128)}, u32[]{:S(2)}) copy-start(f32[16,7168]{1,0:T(8,128)} %param.9) | copy-start | bytes 1376260
  77.3 17.6 %copy-start.1 = (f32[16,7168]{1,0:T(8,128)S(1)}, f32[16,7168]{1,0:T(8,128)}, u32[]{:S(2)}) copy-start(f32[16,7168]{1,0:T(8,128)} %param.8) | copy-start | bytes 1376260
  77.3 17.5 %all-to-all-start.1 = ((f32[8,16,896]{2,1,0:T(8,128)}), f32[8,16,896]{2,1,0:T(8,128)S(1)}, u32[]{:S(2)}, u32[]{:S(2)}) async-start(f32[8,16,896]{2,1,0:T(8,128)} %bitcast.10), calls=%async_computation.1 | async-start | bytes 917504 | tf_op jit(solution)/shard_map/all_to_all | solution.py:99
where the time goes:
time: 96.5 us; the launch traced here: 96.1 us
  blocking collectives  40.4 us (42%)
  waiting for transfers between devices  25.1 us (26%)
  starting transfers between devices  11.8 us (12%)
  other arithmetic  10.4 us (11%)
  local copies, waits for them, and re-layouts  3.04 us (3%)
  between operations  2.75 us (3%)
  matrix products  2.47 us (3%)
    psum x1, blocking collectives, per_device(): sketch = lax.psum(partial_value, ('tensor',) + GROUP)  40.4 us
    all_to_all x1, waiting for transfers between devices, per_device(): held = lax.all_to_all(pieces, GROUP, 0, 0, tiled=True)  12.7 us
    all_to_all x1, waiting for transfers between devices, per_device(): estimate = lax.all_to_all(estimate, GROUP, 0, 0, tiled=True)  12.4 us
    convert_element_type x1, other arithmetic, projection_block(): return (gauss * rank ** (-0.5)).astype(jnp.bfloat16)  9.2 us
    all_to_all x1, starting transfers between devices, per_device(): held = lax.all_to_all(pieces, GROUP, 0, 0, tiled=True)  7.44 us
    all_to_all x1, starting transfers between devices, per_device(): estimate = lax.all_to_all(estimate, GROUP, 0, 0, tiled=True)  4.35 us
  transfers between devices with their start and end apart: 2, of which 2 were waited for; matrix products, arithmetic and copies ran while one was open for 10% of the time, Pallas kernels for 0%

commit v1 on v0

--- a/solution.py
+++ b/solution.py
@@ -89,7 +89,7 @@
         )
         partial_value = term if partial_value is None else partial_value + term
     partial_value = partial_value.reshape(n_fsdp * rows, RANK) * (1.0 / n_rep)
-    sketch = lax.psum(partial_value, ("tensor",) + GROUP)
+    sketch = jnp.sum(jax.lax.all_gather(partial_value, ("tensor",) + GROUP), axis=0)
     sketch_rounded = sketch.astype(jnp.bfloat16)
     estimate = lax.dot_general(
         sketch_rounded, projection, (((1,), (1,)), ((), ())), preferred_element_type=jnp.float32

time: 96.5 us -> 150 us (1.55)
  waiting for transfers between devices: 25.1 us -> 101 us
  blocking collectives: 40.4 us -> 0 us
  between operations: 2.75 us -> 16.2 us
  other arithmetic: 10.4 us -> 14.7 us
    all_gather x0 -> x1, waiting for transfers between devices: none -> 74.5 us  [per_device(): jax.lax.all_gather(partial_value, ('tensor',) + GROUP)]
    psum x1 -> x0, blocking collectives: 40.4 us -> none  [per_device(): sketch = lax.psum(partial_value, ('tensor',) + GROUP)]
    reduce_sum x0 -> x1, other arithmetic: none -> 4.26 us  [per_device(): jnp.sum(jax.lax.all_gather(partial_value, ('tensor',) + GROUP), axis=0)]
  transfers between devices with their start and end apart: 2 -> 3, of which waited for: 2 -> 3; matrix products, arithmetic and copies ran while one was open for 10% -> 7% of each run, Pallas kernels for 0% -> 0%
where the time goes in v1:
time: 150 us; the launch traced here: 149 us
  waiting for transfers between devices  101 us (67%)
  between operations  16.2 us (11%)
  other arithmetic  14.7 us (10%)
  starting transfers between devices  11.5 us (8%)
  matrix products  3.18 us (2%)
  local copies, waits for them, and re-layouts  3.03 us (2%)
    all_gather x1, waiting for transfers between devices, per_device(): jax.lax.all_gather(partial_value, ('tensor',) + GROUP)  74.5 us
    all_to_all x1, waiting for transfers between devices, per_device(): estimate = lax.all_to_all(estimate, GROUP, 0, 0, tiled=True)  13.7 us
    all_to_all x1, waiting for transfers between devices, per_device(): held = lax.all_to_all(pieces, GROUP, 0, 0, tiled=True)  12.6 us
    convert_element_type x1, other arithmetic, projection_block(): return (gauss * rank ** (-0.5)).astype(jnp.bfloat16)  9.2 us
    all_to_all x1, starting transfers between devices, per_device(): held = lax.all_to_all(pieces, GROUP, 0, 0, tiled=True)  7.31 us
    reduce_sum x1, other arithmetic, per_device(): jnp.sum(jax.lax.all_gather(partial_value, ('tensor',) + GROUP), axis=0)  4.26 us
    all_to_all x1, starting transfers between devices, per_device(): estimate = lax.all_to_all(estimate, GROUP, 0, 0, tiled=True)  4.13 us
  transfers between devices with their start and end apart: 3, of which 3 were waited for; matrix products, arithmetic and copies ran while one was open for 7% of the time, Pallas kernels for 0%

profile of v1, /device:TPU:0, one launch (start us, length us, event | category | flops | bytes accessed | tf_op | source)
XLA Modules:
  0.0 149.4 jit_solution(626135453077514456)
XLA Ops:
  7.2 1.3 copy.31
  8.5 0.0 copy-start.2
  8.5 1.1 copy.20
  9.6 7.3 %all-to-all-start = ((bf16[8,64,896]{2,1,0:T(8,128)(2,1)}), bf16[8,64,896]{2,1,0:T(8,128)(2,1)S(1)}, u32[]{:S(2)}, u32[]{:S(2)}) async-start(bf16[8,64,896]{2,1,0:T(8,128)(2,1)} %copy.20), calls=%async_computation | async-start | bytes 1835008 | tf_op jit(solution)/shard_map/all_to_all | solution.py:83
  16.9 0.0 all-gather.2.cloned.1.call-start
  16.9 0.0 copy-done.2
  17.0 0.6 fusion.29
  18.9 9.2 %fusion.18 = bf16[896,512]{1,0:T(8,128)(2,1)S(1)} fusion(s32[]{:T(128)} %bitcast, s32[896]{0:T(1024)S(1)} %add_multiply_fusion), kind=kLoop, calls=%fused_computation.24 | loop fusion | flops 16056320 | bytes 921092 | tf_op jit(solution)/shard_map/convert_element_type | solution.py:35
  28.1 12.6 %all-to-all-done = bf16[8,64,896]{2,1,0:T(8,128)(2,1)S(1)} async-done(((bf16[8,64,896]{2,1,0:T(8,128)(2,1)}), bf16[8,64,896]{2,1,0:T(8,128)(2,1)S(1)}, u32[]{:S(2)}, u32[]{:S(2)}) %all-to-all-start) | async-done | bytes 917536 | tf_op jit(solution)/shard_map/all_to_all | solution.py:83
  40.7 0.3 fusion.23
  41.0 0.3 convolution_add_fusion.2
  41.3 0.3 convolution_add_fusion.1
  41.7 1.0 fusion.19
  42.7 0.0 all-gather.2.cloned.1.call-update
  42.7 74.5 %all-gather.2.cloned.1.call-done = f32[32,128,512]{2,1,0:T(8,128)} async-done(((f32[1,128,512]{2,1,0:T(8,128)}), f32[32,128,512]{2,1,0:T(8,128)}) %all-gather.2.cloned.1.call-update) | async-done | bytes 8388624 | tf_op jit(solution)/shard_map/all_gather | solution.py:92
  117.2 4.3 %reduce_sum.9 = bf16[128,512]{1,0:T(8,128)(2,1)S(1)} reduce(f32[32,128,512]{2,1,0:T(8,128)} %all-gather.2.cloned.1.call-done, f32[]{:T(128)} %constant.67.clone.1), dimensions={0}, to_apply=%region_0.0 | reduce | flops 2031616 | bytes 8519684 | tf_op jit(solution)/shard_map/reduce_sum | solution.py:92
  121.5 0.0 copy-start
  121.5 0.0 copy-start.1
  121.5 1.2 fusion.30
  122.8 4.1 %all-to-all-start.1 = ((f32[8,16,896]{2,1,0:T(8,128)}), f32[8,16,896]{2,1,0:T(8,128)S(1)}, u32[]{:S(2)}, u32[]{:S(2)}) async-start(f32[8,16,896]{2,1,0:T(8,128)} %bitcast.10), calls=%async_computation.1 | async-start | bytes 917504 | tf_op jit(solution)/shard_map/all_to_all | solution.py:99
  127.6 13.7 %all-to-all-done.1 = f32[8,16,896]{2,1,0:T(8,128)S(1)} async-done(((f32[8,16,896]{2,1,0:T(8,128)}), f32[8,16,896]{2,1,0:T(8,128)S(1)}, u32[]{:S(2)}, u32[]{:S(2)}) %all-to-all-start.1) | async-done | bytes 458784 | tf_op jit(solution)/shard_map/all_to_all | solution.py:99
  141.3 0.0 copy-done
  141.3 0.0 copy-done.1
  141.3 1.2 multiply_divide_fusion
  (2 shorter events, 0.0 us)
Async XLA Ops:
  8.5 8.5 %copy-start.2 = (s32[2]{0:T(128)S(1)}, s32[2]{0:T(128)}, u32[]{:S(2)}) copy-start(s32[2]{0:T(128)} %param.6) | copy-start | bytes 28
  9.6 31.1 %all-to-all-start = ((bf16[8,64,896]{2,1,0:T(8,128)(2,1)}), bf16[8,64,896]{2,1,0:T(8,128)(2,1)S(1)}, u32[]{:S(2)}, u32[]{:S(2)}) async-start(bf16[8,64,896]{2,1,0:T(8,128)(2,1)} %copy.20), calls=%async_computation | async-start | bytes 1835008 | tf_op jit(solution)/shard_map/all_to_all | solution.py:83
  16.9 100.3 %all-gather.2.cloned.1.call-start = ((), (), s32[]{:S(2)}) async-start(), calls=%async_computation.2 | async-start | bytes 8650752 | tf_op jit(solution)/shard_map/all_gather | solution.py:92
  121.5 19.8 %copy-start = (f32[16,7168]{1,0:T(8,128)S(1)}, f32[16,7168]{1,0:T(8,128)}, u32[]{:S(2)}) copy-start(f32[16,7168]{1,0:T(8,128)} %param.9) | copy-start | bytes 1376260
  121.5 19.8 %copy-start.1 = (f32[16,7168]{1,0:T(8,128)S(1)}, f32[16,7168]{1,0:T(8,128)}, u32[]{:S(2)}) copy-start(f32[16,7168]{1,0:T(8,128)} %param.8) | copy-start | bytes 1376260
  122.8 18.5 %all-to-all-start.1 = ((f32[8,16,896]{2,1,0:T(8,128)}), f32[8,16,896]{2,1,0:T(8,128)S(1)}, u32[]{:S(2)}, u32[]{:S(2)}) async-start(f32[8,16,896]{2,1,0:T(8,128)} %bitcast.10), calls=%async_computation.1 | async-start | bytes 917504 | tf_op jit(solution)/shard_map/all_to_all | solution.py:99
Sparse Core Ops, SparseCore 0:
  42.8 74.3 all-gather.1
